TPU v7x, 256 devices: a whole 4x4x8 slice. The times are simulated.
256 devices in a mesh: ctx: 16 (over z, core), head: 16 (over y, x).
Axes of the slice: x: 4, y: 4, z: 8, core: 2. Of those that a mesh axis runs over, the one named last changes fastest.
Arguments:
- x_proj: bfloat16 [8192, 8192], P('ctx', 'head'), may hold values from -6 to 6
- z_proj: bfloat16 [8192, 8192], P('ctx', 'head'), may hold values from -6 to 6
- b_proj: bfloat16 [8192, 128], P('ctx'), may hold values from -6 to 6
- c_proj: bfloat16 [8192, 128], P('ctx'), may hold values from -6 to 6
- dt_raw: float32 [128, 8192], P('head', 'ctx'), may hold values from -6 to -2
- a_log: float32 [128], P('head'), may hold values from -11 to 4
- d_skip: float32 [128], P('head'), may hold values from 0.5 to 2
- conv_x: float32 [4, 8192], P(None, 'head'), may hold values from -3 to 3
- conv_bc: float32 [4, 256], replicated, may hold values from -3 to 3
- norm_gain: float32 [8192], P('head'), may hold values from 0.5 to 1.5
- grad_out: bfloat16 [8192, 8192], P('ctx', 'head'), may hold values from -6 to 6
Outputs:
- y_out: bfloat16 [8192, 8192], P('ctx', 'head')
- grad_x: bfloat16 [8192, 8192], P('ctx', 'head')
- grad_z: bfloat16 [8192, 8192], P('ctx', 'head')
- grad_b: bfloat16 [8192, 128], P(('ctx', 'head'))
- grad_c: bfloat16 [8192, 128], P(('ctx', 'head'))
- grad_dt: float32 [128, 8192], P('head', 'ctx')
- grad_alog: float32 [128], P('head')
- grad_dskip: float32 [128], P('head')
- grad_convx: float32 [4, 8192], P(None, 'head')
- grad_convbc: float32 [4, 256], replicated
- grad_gain: float32 [8192], P('head')
All inputs are finite; a program needn't handle non-finite values.
Results may differ from a plain program's by a relative error of at most 0.023.
Values may be sent and summed in bfloat16 or wider, within the bound.
No kernel may reach another device: no remote copies, remote signals or barrier semaphores. Data moves between devices by JAX's collectives and lax.ppermute only.
A program may use at most 64 MiB of HBM per device.

v0:
```python
import jax
import jax.numpy as jnp
from jax import lax
from jax.sharding import PartitionSpec as P

HEADS = 128
HEAD_DIM = 64
GROUP = 256


HIGH = lax.Precision.HIGHEST
EPS = 1e-05


def passed_along(block, axis, distance):
    devices = range(lax.axis_size(axis))
    route = [(i - distance, i) for i in devices if i - distance in devices]
    return lax.ppermute(block, axis, route)


def silu_grad(value):
    sigma = jax.nn.sigmoid(value)
    return sigma * (1.0 + value * (1.0 - sigma))


def tap_sum(padded, weight, count):
    summed = jnp.zeros((count, padded.shape[1]), jnp.float32)
    for offset in range(weight.shape[0]):
        summed = summed + weight[offset][None, :] * padded[offset : offset + count].astype(
            jnp.float32
        )
    return summed


def back_taps(ahead, weight, count):
    final_tap = weight.shape[0] - 1
    summed = jnp.zeros((count, ahead.shape[1]), jnp.float32)
    for offset in range(weight.shape[0]):
        summed = (
            summed
            + weight[offset][None, :] * ahead[final_tap - offset : final_tap - offset + count]
        )
    return summed


def weight_taps(grad_pre, padded, count, tap_count):
    return jnp.stack(
        [
            jnp.sum(grad_pre * padded[offset : offset + count].astype(jnp.float32), axis=0)
            for offset in range(tap_count)
        ]
    )


def decay_table(cum_here):
    size_rows = cum_here.shape[0]
    row_ids = lax.broadcasted_iota(jnp.int32, (size_rows, size_rows), 0)
    col_ids = lax.broadcasted_iota(jnp.int32, (size_rows, size_rows), 1)
    allowed = (col_ids <= row_ids)[:, :, None]
    spread = cum_here[:, None, :] - cum_here[None, :, :]
    return jnp.where(allowed, jnp.exp(jnp.where(allowed, spread, 0.0)), 0.0)


def local(
    x_proj, z_proj, b_proj, c_proj, dt_raw, a_log, d_skip, conv_x, conv_bc, norm_gain, grad_out
):
    length = x_proj.shape[0]
    head_count = dt_raw.shape[0]
    row_width = x_proj.shape[1]
    head_dim = row_width // head_count
    state_dim = b_proj.shape[1]
    tap_count = conv_x.shape[0]
    blocks = length // GROUP
    channels = HEADS * HEAD_DIM
    bc_proj = jnp.concatenate([b_proj, c_proj], axis=1)
    edges = passed_along(
        (x_proj[length - tap_count + 1 :], bc_proj[length - tap_count + 1 :]), "ctx", 1
    )
    x_padded = jnp.concatenate([edges[0], x_proj], axis=0)
    bc_padded = jnp.concatenate([edges[1], bc_proj], axis=0)
    x_pre = tap_sum(x_padded, conv_x, length)
    bc_pre = tap_sum(bc_padded, conv_bc, length)
    x_act = jax.nn.silu(x_pre)
    bc_act = jax.nn.silu(bc_pre)
    decay_rate = jnp.exp(a_log)
    step_size = jax.nn.softplus(dt_raw).T
    x_blocks = x_act.reshape(blocks, GROUP, head_count, head_dim)
    b_blocks = bc_act[:, :state_dim].reshape(blocks, GROUP, state_dim)
    c_blocks = bc_act[:, state_dim:].reshape(blocks, GROUP, state_dim)
    d_blocks = step_size.reshape(blocks, GROUP, head_count)
    cum_blocks = jnp.cumsum(
        (-step_size * decay_rate[None, :]).reshape(blocks, GROUP, head_count), axis=1
    )
    block_ends = cum_blocks[:, -1, :]
    block_decay = jnp.exp(block_ends)
    tail_weight = jnp.exp(cum_blocks[:, -1:, :] - cum_blocks) * d_blocks
    block_states = jnp.einsum(
        "cshp,csn->chpn", tail_weight[..., None] * x_blocks, b_blocks, precision=HIGH
    )

    def fold_blocks(running, inputs):
        decay_now, state_now = inputs
        return (decay_now[:, None, None] * running + state_now, running)

    empty_state = jnp.zeros((head_count, head_dim, state_dim), jnp.float32)
    shard_state, local_entering = lax.scan(fold_blocks, empty_state, (block_decay, block_states))
    prefix_log = jnp.cumsum(block_ends, axis=0) - block_ends
    shard_decay = jnp.exp(jnp.sum(block_ends, axis=0))

    def pass_on(step_index, incoming):
        outgoing = shard_decay[:, None, None] * incoming + shard_state
        return passed_along(outgoing, "ctx", 1)

    entering = lax.fori_loop(0, lax.axis_size("ctx") - 1, pass_on, empty_state)
    block_entry = jnp.exp(prefix_log)[:, :, None, None] * entering[None] + local_entering

    def forward_block(inputs):
        x_here, b_here, c_here, d_here, cum_here, entry = inputs
        decay_map = decay_table(cum_here)
        scores = jnp.dot(c_here, b_here.T, precision=HIGH)
        mixing = scores[:, :, None] * decay_map * d_here[None, :, :]
        inside = jnp.einsum("tsh,shp->thp", mixing, x_here, precision=HIGH)
        carried = jnp.exp(cum_here)[:, :, None] * jnp.einsum(
            "tn,hpn->thp", c_here, entry, precision=HIGH
        )
        return inside + carried

    ssm_blocks = lax.map(
        forward_block, (x_blocks, b_blocks, c_blocks, d_blocks, cum_blocks, block_entry)
    )
    skip_rep = jnp.repeat(d_skip, head_dim)
    ssm_out = ssm_blocks.reshape(length, row_width) + skip_rep[None, :] * x_act
    z_float = z_proj.astype(jnp.float32)
    gate_act = jax.nn.silu(z_float)
    gated_out = ssm_out * gate_act
    grad_float = grad_out.astype(jnp.float32)
    scaled_grad = norm_gain[None, :] * grad_float
    square_sum, cross_sum = lax.psum(
        (jnp.sum(gated_out * gated_out, axis=1), jnp.sum(scaled_grad * gated_out, axis=1)), "head"
    )
    inv_rms = lax.rsqrt(square_sum / channels + EPS)[:, None]
    y_out = (gated_out * inv_rms * norm_gain[None, :]).astype(jnp.bfloat16)
    grad_gain_part = jnp.sum(grad_float * gated_out * inv_rms, axis=0)
    grad_gated = inv_rms * scaled_grad - gated_out * (inv_rms * inv_rms * inv_rms) * (
        cross_sum[:, None] / channels
    )
    grad_ssm = grad_gated * gate_act
    grad_z = (grad_gated * ssm_out * silu_grad(z_float)).astype(jnp.bfloat16)
    grad_skip_part = jnp.sum((grad_ssm * x_act).reshape(length, head_count, head_dim), axis=(0, 2))
    grad_blocks = grad_ssm.reshape(blocks, GROUP, head_count, head_dim)
    local_pull = jnp.einsum(
        "cthp,ctn->chpn", jnp.exp(cum_blocks)[..., None] * grad_blocks, c_blocks, precision=HIGH
    )
    shard_pull = jnp.sum(jnp.exp(prefix_log)[:, :, None, None] * local_pull, axis=0)

    def pass_back(step_index, incoming):
        outgoing = shard_decay[:, None, None] * incoming + shard_pull
        return passed_along(outgoing, "ctx", -1)

    leaving = lax.fori_loop(0, lax.axis_size("ctx") - 1, pass_back, empty_state)
    _, block_exit = lax.scan(fold_blocks, leaving, (block_decay, local_pull), reverse=True)

    def backward_block(inputs):
        x_here, b_here, c_here, d_here, cum_here, entry, exit_grad, grad_here = inputs
        decay_map = decay_table(cum_here)
        scores = jnp.dot(c_here, b_here.T, precision=HIGH)
        weighted = scores[:, :, None] * decay_map
        tail_decay = jnp.exp(cum_here[-1:, :] - cum_here)
        b_exit = jnp.einsum("sn,hpn->shp", b_here, exit_grad, precision=HIGH)
        pulled = (
            jnp.einsum("tsh,thp->shp", weighted, grad_here, precision=HIGH)
            + tail_decay[:, :, None] * b_exit
        )
        grad_x_here = d_here[:, :, None] * pulled
        grad_step = jnp.sum(x_here * pulled, axis=2)
        pair_grad = jnp.einsum("thp,shp->tsh", grad_here, x_here, precision=HIGH)
        masked = pair_grad * decay_map * d_here[None, :, :]
        grad_scores = jnp.sum(masked, axis=2)
        grad_c_here = jnp.dot(grad_scores, b_here, precision=HIGH)
        grad_b_here = jnp.dot(grad_scores.T, c_here, precision=HIGH)
        through = masked * scores[:, :, None]
        grad_cum = jnp.sum(through, axis=1) - jnp.sum(through, axis=0)
        start_map = jnp.exp(cum_here)[:, :, None] * grad_here
        carried = jnp.einsum("tn,hpn->thp", c_here, entry, precision=HIGH)
        grad_cum = grad_cum + jnp.sum(start_map * carried, axis=2)
        grad_c_here = grad_c_here + jnp.einsum("thp,hpn->tn", start_map, entry, precision=HIGH)
        release = tail_decay * d_here * jnp.sum(x_here * b_exit, axis=2)
        grad_cum = grad_cum - release
        end_total = jnp.sum(release, axis=0) + jnp.exp(cum_here[-1]) * jnp.sum(
            entry * exit_grad, axis=(1, 2)
        )
        grad_cum = jnp.concatenate([grad_cum[:-1], grad_cum[-1:] + end_total[None, :]], axis=0)
        grad_log = jnp.flip(jnp.cumsum(jnp.flip(grad_cum, 0), axis=0), 0)
        grad_b_here = grad_b_here + jnp.einsum(
            "shp,hpn->sn", (tail_decay * d_here)[:, :, None] * x_here, exit_grad, precision=HIGH
        )
        return (grad_x_here, grad_b_here, grad_c_here, grad_step, grad_log)

    grad_x_blocks, grad_b_blocks, grad_c_blocks, grad_step_blocks, grad_log_blocks = lax.map(
        backward_block,
        (x_blocks, b_blocks, c_blocks, d_blocks, cum_blocks, block_entry, block_exit, grad_blocks),
    )
    grad_log_rows = grad_log_blocks.reshape(length, head_count)
    grad_step_rows = (
        grad_step_blocks.reshape(length, head_count) - decay_rate[None, :] * grad_log_rows
    )
    grad_alog_part = decay_rate * -jnp.sum(step_size * grad_log_rows, axis=0)
    grad_dt = (grad_step_rows * jax.nn.sigmoid(dt_raw).T).T
    grad_x_act = grad_x_blocks.reshape(length, row_width) + skip_rep[None, :] * grad_ssm
    grad_bc_act = jnp.concatenate(
        [grad_b_blocks.reshape(length, state_dim), grad_c_blocks.reshape(length, state_dim)], axis=1
    )
    grad_x_pre = grad_x_act * silu_grad(x_pre)
    grad_bc_pre = grad_bc_act * silu_grad(bc_pre)
    ahead = passed_along((grad_x_pre[: tap_count - 1], grad_bc_pre[: tap_count - 1]), "ctx", -1)
    x_ahead = jnp.concatenate([grad_x_pre, ahead[0]], axis=0)
    bc_ahead = jnp.concatenate([grad_bc_pre, ahead[1]], axis=0)
    grad_x = back_taps(x_ahead, conv_x, length).astype(jnp.bfloat16)
    bc_back = back_taps(bc_ahead, conv_bc, length)
    shares = lax.psum_scatter(bc_back, "head", scatter_dimension=0, tiled=True)
    grad_b = shares[:, :state_dim].astype(jnp.bfloat16)
    grad_c = shares[:, state_dim:].astype(jnp.bfloat16)
    grad_convx_part = weight_taps(grad_x_pre, x_padded, length, tap_count)
    grad_convbc_part = weight_taps(grad_bc_pre, bc_padded, length, tap_count)
    grad_alog, grad_dskip, grad_convx, grad_gain = lax.psum(
        (grad_alog_part, grad_skip_part, grad_convx_part, grad_gain_part), "ctx"
    )
    grad_convbc = lax.psum(grad_convbc_part, ("ctx", "head"))
    return (
        y_out,
        grad_x,
        grad_z,
        grad_b,
        grad_c,
        grad_dt,
        grad_alog,
        grad_dskip,
        grad_convx,
        grad_convbc,
        grad_gain,
    )


def solution(mesh):
    return jax.shard_map(
        local,
        mesh=mesh,
        in_specs=(
            P("ctx", "head"),
            P("ctx", "head"),
            P("ctx", None),
            P("ctx", None),
            P("head", "ctx"),
            P("head"),
            P("head"),
            P(None, "head"),
            P(),
            P("head"),
            P("ctx", "head"),
        ),
        out_specs=(
            P("ctx", "head"),
            P("ctx", "head"),
            P("ctx", "head"),
            P(("ctx", "head"), None),
            P(("ctx", "head"), None),
            P("head", "ctx"),
            P("head"),
            P("head"),
            P(None, "head"),
            P(),
            P("head"),
        ),
        check_vma=False,
    )
```

profile of v0, /device:TPU:1, one launch (start us, length us, event | category | flops | bytes accessed | tf_op | source)
XLA Modules:
  0.0 672.7 jit_solution(3489720683614918270)
XLA Ops:
  35.6 116.3 %while.77 = (s32[]{:T(128)}, f32[8,64,128]{2,1,0:T(8,128)S(1)}, f32[8]{0:T(128)S(1)}, f32[8,64,128]{2,1,0:T(8,128)S(1)}, s32[]{:T(128)}) while((s32[]{:T(128)}, f32[8,64,128]{2,1,0:T(8,128)S(1)}, f32[8]{0:T(128)S(1)}, f32[8,64,128]{2,1,0:T(8,128)S(1)}, s32[]{:T(128)}) %tuple.173), condition=%wide.region_7.8_spmd, body=%wide.region_6.7_spmd.sunk | while | flops 131074 | bytes 1835141 | solution.py:114
  153.4 36.2 %while.78 = (s32[]{:T(128)}, f32[2,256,8,64]{1,0,3,2:T(2,128)}, f32[2,256,8,64]{1,3,2,0:T(8,128)}, f32[2,256,128]{2,1,0:T(8,128)S(1)}, f32[2,256,128]{2,1,0:T(8,...) while((s32[]{:T(128)}, f32[2,256,8,64]{1,0,3,2:T(2,128)}, ...), condition=%wide.region_9.10_spmd, body=%wide.region_8.9_spmd.sunk | while | flops 707592192 | bytes 5580925 | solution.py:128
  160.0 11.5 %dynamic_update_slice.48 = f32[2,256,8,64]{1,0,3,2:T(2,128)} dynamic-update-slice(f32[2,256,8,64]{1,0,3,2:T(2,128)} %get-tuple-element.953, f32[1,256,8,64]{1,0,3,2:T(1,128)S(1)} %copy.218, s32[]{:T(128)S(6)} %copy.254, s32[]{:T(128)} %constant.125.clone.1..sunk, s32[]{:T(128)} %constant.125.clone.1..sunk, s32[]{:T(128)} %constant.125.clone.1..sunk) | dynamic-update-slice | bytes 1048580 | tf_op jit(solution)/shard_map/while/body/jit(dynamic_update_index_in_dim)/dynamic_update_slice | solution.py:128
  178.1 11.5 %dynamic_update_slice.48 = f32[2,256,8,64]{1,0,3,2:T(2,128)} dynamic-update-slice(f32[2,256,8,64]{1,0,3,2:T(2,128)} %get-tuple-element.953, f32[1,256,8,64]{1,0,3,2:T(1,128)S(1)} %copy.218, s32[]{:T(128)S(6)} %copy.254, s32[]{:T(128)} %constant.125.clone.1..sunk, s32[]{:T(128)} %constant.125.clone.1..sunk, s32[]{:T(128)} %constant.125.clone.1..sunk) | dynamic-update-slice | bytes 1048580 | tf_op jit(solution)/shard_map/while/body/jit(dynamic_update_index_in_dim)/dynamic_update_slice | solution.py:128
  192.0 33.5 %psum.49 = f32[512]{0:T(512)S(1)} all-reduce(f32[512]{0:T(512)S(1)} %get-tuple-element.601), channel_id=1, replica_groups=mesh['ctx'=16,'head'=16] {'head'}, use_global_device_ids=true, to_apply=%region_11.12 | all-reduce | flops 512 | bytes 4096 | tf_op jit(solution)/shard_map/psum | solution.py:138
  227.5 28.9 %psum.50 = f32[512]{0:T(512)S(1)} all-reduce(f32[512]{0:T(512)S(1)} %get-tuple-element.496), channel_id=1, replica_groups=mesh['ctx'=16,'head'=16] {'head'}, use_global_device_ids=true, to_apply=%region_13.14 | all-reduce | flops 512 | bytes 4096 | tf_op jit(solution)/shard_map/psum | solution.py:138
  263.5 146.2 %while.79 = (s32[]{:T(128)}, f32[8,64,128]{2,1,0:T(8,128)S(1)}, f32[8]{0:T(128)S(1)}, f32[8,64,128]{2,1,0:T(8,128)S(1)}, s32[]{:T(128)}) while((s32[]{:T(128)}, f32[8,64,128]{2,1,0:T(8,128)S(1)}, f32[8]{0:T(128)S(1)}, f32[8,64,128]{2,1,0:T(8,128)S(1)}, s32[]{:T(128)}) %tuple.195), condition=%wide.region_16.17_spmd, body=%wide.region_15.16_spmd.sunk | while | flops 131074 | bytes 1835141 | solution.py:160
  263.6 11.7 %collective-permute-start.1 = (f32[8,64,128]{2,1,0:T(8,128)S(1)}, f32[8,64,128]{2,1,0:T(8,128)S(1)}, u32[]{:S(2)}, u32[]{:S(2)}) collective-permute-start(f32[8,64,128]{2,1,0:T(8,128)S(1)} %multiply_add_fusion.7), channel_id=1, source_target_pairs={{16,0},{32,16},{48,32},{64,48},{80,64},{96,80},{112,96},{128,112},... | collective-permute-start | bytes 786440 | tf_op jit(solution)/shard_map/while/body/eval_jaxpr/ppermute | solution.py:18
  275.3 10.6 %collective-permute-done.1 = f32[8,64,128]{2,1,0:T(8,128)S(1)} collective-permute-done((f32[8,64,128]{2,1,0:T(8,128)S(1)}, f32[8,64,128]{2,1,0:T(8,128)S(1)}, u32[]{:S(2)}, u32[]{:S(2)}) %collective-permute-start.1) | collective-permute-done | bytes 262176 | tf_op jit(solution)/shard_map/while/body/eval_jaxpr/ppermute | solution.py:18
  311.3 7.8 %collective-permute-done.1 = f32[8,64,128]{2,1,0:T(8,128)S(1)} collective-permute-done((f32[8,64,128]{2,1,0:T(8,128)S(1)}, f32[8,64,128]{2,1,0:T(8,128)S(1)}, u32[]{:S(2)}, u32[]{:S(2)}) %collective-permute-start.1) | collective-permute-done | bytes 262176 | tf_op jit(solution)/shard_map/while/body/eval_jaxpr/ppermute | solution.py:18
  328.9 8.8 %collective-permute-done.1 = f32[8,64,128]{2,1,0:T(8,128)S(1)} collective-permute-done((f32[8,64,128]{2,1,0:T(8,128)S(1)}, f32[8,64,128]{2,1,0:T(8,128)S(1)}, u32[]{:S(2)}, u32[]{:S(2)}) %collective-permute-start.1) | collective-permute-done | bytes 262176 | tf_op jit(solution)/shard_map/while/body/eval_jaxpr/ppermute | solution.py:18
  339.7 7.0 %collective-permute-done.1 = f32[8,64,128]{2,1,0:T(8,128)S(1)} collective-permute-done((f32[8,64,128]{2,1,0:T(8,128)S(1)}, f32[8,64,128]{2,1,0:T(8,128)S(1)}, u32[]{:S(2)}, u32[]{:S(2)}) %collective-permute-start.1) | collective-permute-done | bytes 262176 | tf_op jit(solution)/shard_map/while/body/eval_jaxpr/ppermute | solution.py:18
  348.7 7.0 %collective-permute-done.1 = f32[8,64,128]{2,1,0:T(8,128)S(1)} collective-permute-done((f32[8,64,128]{2,1,0:T(8,128)S(1)}, f32[8,64,128]{2,1,0:T(8,128)S(1)}, u32[]{:S(2)}, u32[]{:S(2)}) %collective-permute-start.1) | collective-permute-done | bytes 262176 | tf_op jit(solution)/shard_map/while/body/eval_jaxpr/ppermute | solution.py:18
  357.7 7.0 %collective-permute-done.1 = f32[8,64,128]{2,1,0:T(8,128)S(1)} collective-permute-done((f32[8,64,128]{2,1,0:T(8,128)S(1)}, f32[8,64,128]{2,1,0:T(8,128)S(1)}, u32[]{:S(2)}, u32[]{:S(2)}) %collective-permute-start.1) | collective-permute-done | bytes 262176 | tf_op jit(solution)/shard_map/while/body/eval_jaxpr/ppermute | solution.py:18
  366.7 7.0 %collective-permute-done.1 = f32[8,64,128]{2,1,0:T(8,128)S(1)} collective-permute-done((f32[8,64,128]{2,1,0:T(8,128)S(1)}, f32[8,64,128]{2,1,0:T(8,128)S(1)}, u32[]{:S(2)}, u32[]{:S(2)}) %collective-permute-start.1) | collective-permute-done | bytes 262176 | tf_op jit(solution)/shard_map/while/body/eval_jaxpr/ppermute | solution.py:18
  375.7 7.0 %collective-permute-done.1 = f32[8,64,128]{2,1,0:T(8,128)S(1)} collective-permute-done((f32[8,64,128]{2,1,0:T(8,128)S(1)}, f32[8,64,128]{2,1,0:T(8,128)S(1)}, u32[]{:S(2)}, u32[]{:S(2)}) %collective-permute-start.1) | collective-permute-done | bytes 262176 | tf_op jit(solution)/shard_map/while/body/eval_jaxpr/ppermute | solution.py:18
  384.7 7.0 %collective-permute-done.1 = f32[8,64,128]{2,1,0:T(8,128)S(1)} collective-permute-done((f32[8,64,128]{2,1,0:T(8,128)S(1)}, f32[8,64,128]{2,1,0:T(8,128)S(1)}, u32[]{:S(2)}, u32[]{:S(2)}) %collective-permute-start.1) | collective-permute-done | bytes 262176 | tf_op jit(solution)/shard_map/while/body/eval_jaxpr/ppermute | solution.py:18
  393.7 7.0 %collective-permute-done.1 = f32[8,64,128]{2,1,0:T(8,128)S(1)} collective-permute-done((f32[8,64,128]{2,1,0:T(8,128)S(1)}, f32[8,64,128]{2,1,0:T(8,128)S(1)}, u32[]{:S(2)}, u32[]{:S(2)}) %collective-permute-start.1) | collective-permute-done | bytes 262176 | tf_op jit(solution)/shard_map/while/body/eval_jaxpr/ppermute | solution.py:18
  402.7 7.0 %collective-permute-done.1 = f32[8,64,128]{2,1,0:T(8,128)S(1)} collective-permute-done((f32[8,64,128]{2,1,0:T(8,128)S(1)}, f32[8,64,128]{2,1,0:T(8,128)S(1)}, u32[]{:S(2)}, u32[]{:S(2)}) %collective-permute-start.1) | collective-permute-done | bytes 262176 | tf_op jit(solution)/shard_map/while/body/eval_jaxpr/ppermute | solution.py:18
  411.4 87.2 %while.81 = (s32[]{:T(128)}, f32[2,256,8,64]{1,0,3,2:T(2,128)}, f32[2,256,128]{2,1,0:T(8,128)}, f32[2,256,128]{2,1,0:T(8,128)}, f32[2,256,8]{1,2,0:T(8,128)}, /*...) while((s32[]{:T(128)}, f32[2,256,8,64]{1,0,3,2:T(2,128)}, ...), condition=%wide.region_30.31_spmd, body=%wide.region_19.30_spmd.sunk | while | flops 1921460224 | bytes 14728557 | solution.py:199
  443.5 11.5 %dynamic_update_slice.53 = f32[2,256,8,64]{1,0,3,2:T(2,128)} dynamic-update-slice(f32[2,256,8,64]{1,0,3,2:T(2,128)} %get-tuple-element.1024, f32[1,256,8,64]{1,0,3,2:T(1,128)S(1)} %copy.224, s32[]{:T(128)S(6)} %copy.279, s32[]{:T(128)} %constant.125.clone.1..sunk.1, s32[]{:T(128)} %constant.125.clone.1..sunk.1, s32[]{:T(128)} %constant.125.clone.1..sunk.1) | dynamic-update-slice | bytes 1048580 | tf_op jit(solution)/shard_map/while/body/jit(dynamic_update_index_in_dim)/dynamic_update_slice | solution.py:128
  487.1 11.5 %dynamic_update_slice.53 = f32[2,256,8,64]{1,0,3,2:T(2,128)} dynamic-update-slice(f32[2,256,8,64]{1,0,3,2:T(2,128)} %get-tuple-element.1024, f32[1,256,8,64]{1,0,3,2:T(1,128)S(1)} %copy.224, s32[]{:T(128)S(6)} %copy.279, s32[]{:T(128)} %constant.125.clone.1..sunk.1, s32[]{:T(128)} %constant.125.clone.1..sunk.1, s32[]{:T(128)} %constant.125.clone.1..sunk.1) | dynamic-update-slice | bytes 1048580 | tf_op jit(solution)/shard_map/while/body/jit(dynamic_update_index_in_dim)/dynamic_update_slice | solution.py:128
  515.5 62.7 %all-reduce = (f32[8]{0:T(128)}, f32[8]{0:T(128)}, f32[4,512]{1,0:T(4,128)}, f32[512]{0:T(512)}) all-reduce(f32[8]{0:T(128)S(1)} %negate_multiply_fusion, f32[8]{0:T(128)S(1)} %reduce_sum.225, f32[4,512]{1,0:T(4,128)S(1)} %pad_maximum_fusion.5, f32[512]{0:T(512)S(1)} %copy-done.40), channel_id=1, replica_groups=mesh['ctx'=16,'head'=16] {'ctx'}, use_global_device_ids=true, to_apply=%region_33.34 | all-reduce | flops 2576 | bytes 20608 | tf_op jit(solution)/shard_map/psum | solution.py:225
  581.2 80.8 %psum.54 = f32[4,256]{1,0:T(4,128)} all-reduce(f32[4,256]{1,0:T(4,128)S(1)} %pad_maximum_fusion.6), channel_id=1, replica_groups=mesh['ctx'=16,'head'=16] {'ctx','head'}, use_global_device_ids=true, to_apply=%region_46.47 | all-reduce | flops 1024 | bytes 8192 | tf_op jit(solution)/shard_map/psum | solution.py:228
  (348 shorter events, 311.2 us)
Async XLA Ops:
  7.2 657.3 %reduce-scatter.2.cloned.1.call-start = ((), (), s32[]{:S(2)}) async-start(), calls=%async_computation.1 | async-start | bytes 557056 | tf_op jit(solution)/shard_map/reduce_scatter | solution.py:220
  8.2 20.1 %collective-permute-start.2 = (bf16[3,512]{0,1:T(8,128)(2,1)S(1)}, bf16[3,512]{0,1:T(8,128)(2,1)S(1)}, u32[]{:S(2)}, u32[]{:S(2)}) collective-permute-start(bf16[3,512]{0,1:T(8,128)(2,1)S(1)} %copy.135), channel_id=1, source_target_pairs={{0,16},{16,32},{32,48},{48,64},{64,80},{80,96},{96,112},{112,128},... | collective-permute-start | bytes 9224 | tf_op jit(solution)/shard_map/ppermute | solution.py:18
  15.0 12.9 %collective-permute-start.3 = (bf16[3,256]{1,0:T(4,128)(2,1)S(1)}, bf16[3,256]{1,0:T(4,128)(2,1)S(1)}, u32[]{:S(2)}, u32[]{:S(2)}) collective-permute-start(bf16[3,256]{1,0:T(4,128)(2,1)S(1)} %slice.165), channel_id=1, source_target_pairs={{0,16},{16,32},{32,48},{48,64},{64,80},{80,96},{96,112},{112,128},... | collective-permute-start | bytes 4616 | tf_op jit(solution)/shard_map/ppermute | solution.py:18
  43.0 7.7 %collective-permute-start = (f32[8,64,128]{2,1,0:T(8,128)S(1)}, f32[8,64,128]{2,1,0:T(8,128)S(1)}, u32[]{:S(2)}, u32[]{:S(2)}) collective-permute-start(f32[8,64,128]{2,1,0:T(8,128)S(1)} %multiply_add_fusion.6), channel_id=1, source_target_pairs={{0,16},{16,32},{32,48},{48,64},{64,80},{80,96},{96,112},{112,128},... | collective-permute-start | bytes 786440 | tf_op jit(solution)/shard_map/while/body/eval_jaxpr/ppermute | solution.py:18
  50.8 7.7 %collective-permute-start = (f32[8,64,128]{2,1,0:T(8,128)S(1)}, f32[8,64,128]{2,1,0:T(8,128)S(1)}, u32[]{:S(2)}, u32[]{:S(2)}) collective-permute-start(f32[8,64,128]{2,1,0:T(8,128)S(1)} %multiply_add_fusion.6), channel_id=1, source_target_pairs={{0,16},{16,32},{32,48},{48,64},{64,80},{80,96},{96,112},{112,128},... | collective-permute-start | bytes 786440 | tf_op jit(solution)/shard_map/while/body/eval_jaxpr/ppermute | solution.py:18
  58.6 7.7 %collective-permute-start = (f32[8,64,128]{2,1,0:T(8,128)S(1)}, f32[8,64,128]{2,1,0:T(8,128)S(1)}, u32[]{:S(2)}, u32[]{:S(2)}) collective-permute-start(f32[8,64,128]{2,1,0:T(8,128)S(1)} %multiply_add_fusion.6), channel_id=1, source_target_pairs={{0,16},{16,32},{32,48},{48,64},{64,80},{80,96},{96,112},{112,128},... | collective-permute-start | bytes 786440 | tf_op jit(solution)/shard_map/while/body/eval_jaxpr/ppermute | solution.py:18
  66.4 7.7 %collective-permute-start = (f32[8,64,128]{2,1,0:T(8,128)S(1)}, f32[8,64,128]{2,1,0:T(8,128)S(1)}, u32[]{:S(2)}, u32[]{:S(2)}) collective-permute-start(f32[8,64,128]{2,1,0:T(8,128)S(1)} %multiply_add_fusion.6), channel_id=1, source_target_pairs={{0,16},{16,32},{32,48},{48,64},{64,80},{80,96},{96,112},{112,128},... | collective-permute-start | bytes 786440 | tf_op jit(solution)/shard_map/while/body/eval_jaxpr/ppermute | solution.py:18
  74.2 7.7 %collective-permute-start = (f32[8,64,128]{2,1,0:T(8,128)S(1)}, f32[8,64,128]{2,1,0:T(8,128)S(1)}, u32[]{:S(2)}, u32[]{:S(2)}) collective-permute-start(f32[8,64,128]{2,1,0:T(8,128)S(1)} %multiply_add_fusion.6), channel_id=1, source_target_pairs={{0,16},{16,32},{32,48},{48,64},{64,80},{80,96},{96,112},{112,128},... | collective-permute-start | bytes 786440 | tf_op jit(solution)/shard_map/while/body/eval_jaxpr/ppermute | solution.py:18
  82.0 7.7 %collective-permute-start = (f32[8,64,128]{2,1,0:T(8,128)S(1)}, f32[8,64,128]{2,1,0:T(8,128)S(1)}, u32[]{:S(2)}, u32[]{:S(2)}) collective-permute-start(f32[8,64,128]{2,1,0:T(8,128)S(1)} %multiply_add_fusion.6), channel_id=1, source_target_pairs={{0,16},{16,32},{32,48},{48,64},{64,80},{80,96},{96,112},{112,128},... | collective-permute-start | bytes 786440 | tf_op jit(solution)/shard_map/while/body/eval_jaxpr/ppermute | solution.py:18
  89.8 7.7 %collective-permute-start = (f32[8,64,128]{2,1,0:T(8,128)S(1)}, f32[8,64,128]{2,1,0:T(8,128)S(1)}, u32[]{:S(2)}, u32[]{:S(2)}) collective-permute-start(f32[8,64,128]{2,1,0:T(8,128)S(1)} %multiply_add_fusion.6), channel_id=1, source_target_pairs={{0,16},{16,32},{32,48},{48,64},{64,80},{80,96},{96,112},{112,128},... | collective-permute-start | bytes 786440 | tf_op jit(solution)/shard_map/while/body/eval_jaxpr/ppermute | solution.py:18
  97.5 7.7 %collective-permute-start = (f32[8,64,128]{2,1,0:T(8,128)S(1)}, f32[8,64,128]{2,1,0:T(8,128)S(1)}, u32[]{:S(2)}, u32[]{:S(2)}) collective-permute-start(f32[8,64,128]{2,1,0:T(8,128)S(1)} %multiply_add_fusion.6), channel_id=1, source_target_pairs={{0,16},{16,32},{32,48},{48,64},{64,80},{80,96},{96,112},{112,128},... | collective-permute-start | bytes 786440 | tf_op jit(solution)/shard_map/while/body/eval_jaxpr/ppermute | solution.py:18
  105.3 7.7 %collective-permute-start = (f32[8,64,128]{2,1,0:T(8,128)S(1)}, f32[8,64,128]{2,1,0:T(8,128)S(1)}, u32[]{:S(2)}, u32[]{:S(2)}) collective-permute-start(f32[8,64,128]{2,1,0:T(8,128)S(1)} %multiply_add_fusion.6), channel_id=1, source_target_pairs={{0,16},{16,32},{32,48},{48,64},{64,80},{80,96},{96,112},{112,128},... | collective-permute-start | bytes 786440 | tf_op jit(solution)/shard_map/while/body/eval_jaxpr/ppermute | solution.py:18
  263.6 22.3 %collective-permute-start.1 = (f32[8,64,128]{2,1,0:T(8,128)S(1)}, f32[8,64,128]{2,1,0:T(8,128)S(1)}, u32[]{:S(2)}, u32[]{:S(2)}) collective-permute-start(f32[8,64,128]{2,1,0:T(8,128)S(1)} %multiply_add_fusion.7), channel_id=1, source_target_pairs={{16,0},{32,16},{48,32},{64,48},{80,64},{96,80},{112,96},{128,112},... | collective-permute-start | bytes 786440 | tf_op jit(solution)/shard_map/while/body/eval_jaxpr/ppermute | solution.py:18
  309.3 9.7 %collective-permute-start.1 = (f32[8,64,128]{2,1,0:T(8,128)S(1)}, f32[8,64,128]{2,1,0:T(8,128)S(1)}, u32[]{:S(2)}, u32[]{:S(2)}) collective-permute-start(f32[8,64,128]{2,1,0:T(8,128)S(1)} %multiply_add_fusion.7), channel_id=1, source_target_pairs={{16,0},{32,16},{48,32},{64,48},{80,64},{96,80},{112,96},{128,112},... | collective-permute-start | bytes 786440 | tf_op jit(solution)/shard_map/while/body/eval_jaxpr/ppermute | solution.py:18
  327.0 10.7 %collective-permute-start.1 = (f32[8,64,128]{2,1,0:T(8,128)S(1)}, f32[8,64,128]{2,1,0:T(8,128)S(1)}, u32[]{:S(2)}, u32[]{:S(2)}) collective-permute-start(f32[8,64,128]{2,1,0:T(8,128)S(1)} %multiply_add_fusion.7), channel_id=1, source_target_pairs={{16,0},{32,16},{48,32},{64,48},{80,64},{96,80},{112,96},{128,112},... | collective-permute-start | bytes 786440 | tf_op jit(solution)/shard_map/while/body/eval_jaxpr/ppermute | solution.py:18
  337.8 8.9 %collective-permute-start.1 = (f32[8,64,128]{2,1,0:T(8,128)S(1)}, f32[8,64,128]{2,1,0:T(8,128)S(1)}, u32[]{:S(2)}, u32[]{:S(2)}) collective-permute-start(f32[8,64,128]{2,1,0:T(8,128)S(1)} %multiply_add_fusion.7), channel_id=1, source_target_pairs={{16,0},{32,16},{48,32},{64,48},{80,64},{96,80},{112,96},{128,112},... | collective-permute-start | bytes 786440 | tf_op jit(solution)/shard_map/while/body/eval_jaxpr/ppermute | solution.py:18
  346.8 8.9 %collective-permute-start.1 = (f32[8,64,128]{2,1,0:T(8,128)S(1)}, f32[8,64,128]{2,1,0:T(8,128)S(1)}, u32[]{:S(2)}, u32[]{:S(2)}) collective-permute-start(f32[8,64,128]{2,1,0:T(8,128)S(1)} %multiply_add_fusion.7), channel_id=1, source_target_pairs={{16,0},{32,16},{48,32},{64,48},{80,64},{96,80},{112,96},{128,112},... | collective-permute-start | bytes 786440 | tf_op jit(solution)/shard_map/while/body/eval_jaxpr/ppermute | solution.py:18
  355.8 8.9 %collective-permute-start.1 = (f32[8,64,128]{2,1,0:T(8,128)S(1)}, f32[8,64,128]{2,1,0:T(8,128)S(1)}, u32[]{:S(2)}, u32[]{:S(2)}) collective-permute-start(f32[8,64,128]{2,1,0:T(8,128)S(1)} %multiply_add_fusion.7), channel_id=1, source_target_pairs={{16,0},{32,16},{48,32},{64,48},{80,64},{96,80},{112,96},{128,112},... | collective-permute-start | bytes 786440 | tf_op jit(solution)/shard_map/while/body/eval_jaxpr/ppermute | solution.py:18
  364.8 8.9 %collective-permute-start.1 = (f32[8,64,128]{2,1,0:T(8,128)S(1)}, f32[8,64,128]{2,1,0:T(8,128)S(1)}, u32[]{:S(2)}, u32[]{:S(2)}) collective-permute-start(f32[8,64,128]{2,1,0:T(8,128)S(1)} %multiply_add_fusion.7), channel_id=1, source_target_pairs={{16,0},{32,16},{48,32},{64,48},{80,64},{96,80},{112,96},{128,112},... | collective-permute-start | bytes 786440 | tf_op jit(solution)/shard_map/while/body/eval_jaxpr/ppermute | solution.py:18
  373.8 8.9 %collective-permute-start.1 = (f32[8,64,128]{2,1,0:T(8,128)S(1)}, f32[8,64,128]{2,1,0:T(8,128)S(1)}, u32[]{:S(2)}, u32[]{:S(2)}) collective-permute-start(f32[8,64,128]{2,1,0:T(8,128)S(1)} %multiply_add_fusion.7), channel_id=1, source_target_pairs={{16,0},{32,16},{48,32},{64,48},{80,64},{96,80},{112,96},{128,112},... | collective-permute-start | bytes 786440 | tf_op jit(solution)/shard_map/while/body/eval_jaxpr/ppermute | solution.py:18
  382.8 8.9 %collective-permute-start.1 = (f32[8,64,128]{2,1,0:T(8,128)S(1)}, f32[8,64,128]{2,1,0:T(8,128)S(1)}, u32[]{:S(2)}, u32[]{:S(2)}) collective-permute-start(f32[8,64,128]{2,1,0:T(8,128)S(1)} %multiply_add_fusion.7), channel_id=1, source_target_pairs={{16,0},{32,16},{48,32},{64,48},{80,64},{96,80},{112,96},{128,112},... | collective-permute-start | bytes 786440 | tf_op jit(solution)/shard_map/while/body/eval_jaxpr/ppermute | solution.py:18
  391.8 8.9 %collective-permute-start.1 = (f32[8,64,128]{2,1,0:T(8,128)S(1)}, f32[8,64,128]{2,1,0:T(8,128)S(1)}, u32[]{:S(2)}, u32[]{:S(2)}) collective-permute-start(f32[8,64,128]{2,1,0:T(8,128)S(1)} %multiply_add_fusion.7), channel_id=1, source_target_pairs={{16,0},{32,16},{48,32},{64,48},{80,64},{96,80},{112,96},{128,112},... | collective-permute-start | bytes 786440 | tf_op jit(solution)/shard_map/while/body/eval_jaxpr/ppermute | solution.py:18
  400.8 8.9 %collective-permute-start.1 = (f32[8,64,128]{2,1,0:T(8,128)S(1)}, f32[8,64,128]{2,1,0:T(8,128)S(1)}, u32[]{:S(2)}, u32[]{:S(2)}) collective-permute-start(f32[8,64,128]{2,1,0:T(8,128)S(1)} %multiply_add_fusion.7), channel_id=1, source_target_pairs={{16,0},{32,16},{48,32},{64,48},{80,64},{96,80},{112,96},{128,112},... | collective-permute-start | bytes 786440 | tf_op jit(solution)/shard_map/while/body/eval_jaxpr/ppermute | solution.py:18
  512.4 149.7 %collective-permute-start.4 = (f32[3,512]{0,1:T(8,128)S(1)}, f32[3,512]{0,1:T(8,128)S(1)}, u32[]{:S(2)}, u32[]{:S(2)}) collective-permute-start(f32[3,512]{0,1:T(8,128)S(1)} %slice.175), channel_id=1, source_target_pairs={{16,0},{32,16},{48,32},{64,48},{80,64},{96,80},{112,96},{128,112},... | collective-permute-start | bytes 18440 | tf_op jit(solution)/shard_map/ppermute | solution.py:18
  (56 other events, 1282.5 us)
Sparse Core Ops, SparseCore 0:
  508.5 93.7 reduce-scatter.1
where the time goes:
time: 679 us; the launch traced here: 673 us
  blocking collectives  206 us (30%)
  waiting for transfers between devices  159 us (23%)
  starting transfers between devices  115 us (17%)
  local copies, waits for them, and re-layouts  93.2 us (14%)
  other arithmetic  42.8 us (6%)
  matrix products  41.9 us (6%)
  between operations  14.8 us (2%)
    ppermute x34, waiting for transfers between devices, passed_along(): return lax.ppermute(block, axis, route)  159 us
    ppermute x34, starting transfers between devices, passed_along(): return lax.ppermute(block, axis, route)  115 us
    psum x1, blocking collectives, local(): grad_convbc = lax.psum(grad_convbc_part, ('ctx', 'head'))  80.8 us
    psum x1, blocking collectives, local(): lax.psum((grad_alog_part, grad_skip_part, grad_convx_part, grad_gain_part...  62.7 us
    psum x2, blocking collectives, local(): lax.psum((jnp.sum(gated_out * gated_out, axis=1), jnp.sum(scaled_grad * g...  62.4 us
    dynamic_update_slice x8, local copies, waits for them, and re-layouts, local(): lax.map(forward_block, (x_blocks, b_blocks, c_blocks, d_blocks, cum_block...  48.2 us
  transfers between devices with their start and end apart: 35, of which 31 were waited for; matrix products, arithmetic and copies ran while one was open for 4% of the time, Pallas kernels for 0%

commit v1 on v0

v1 whole, which is shorter than its diff:
```python
import jax
import jax.numpy as jnp
from jax import lax
from jax.sharding import PartitionSpec as P

HEADS = 128
HEAD_DIM = 64
GROUP = 256


HIGH = lax.Precision.HIGHEST
EPS = 1e-05


def passed_along(block, axis, distance):
    devices = range(lax.axis_size(axis))
    route = [(i - distance, i) for i in devices if i - distance in devices]
    return lax.ppermute(block, axis, route)


def exclusive_scan(decay, state, axis, direction):
    count = lax.axis_size(axis)
    inc_decay, inc_state = decay, state
    exc_decay = jnp.ones_like(decay)
    exc_state = jnp.zeros_like(state)
    distance = 1
    while distance < count:
        got_decay, got_state = passed_along((inc_decay, inc_state), axis, distance * direction)
        exc_state = exc_decay[:, None, None] * got_state + exc_state
        exc_decay = exc_decay * got_decay
        if 2 * distance < count:
            inc_state = inc_decay[:, None, None] * got_state + inc_state
            inc_decay = inc_decay * got_decay
        distance *= 2
    return exc_state


def silu_grad(value):
    sigma = jax.nn.sigmoid(value)
    return sigma * (1.0 + value * (1.0 - sigma))


def tap_sum(padded, weight, count):
    summed = jnp.zeros((count, padded.shape[1]), jnp.float32)
    for offset in range(weight.shape[0]):
        summed = summed + weight[offset][None, :] * padded[offset : offset + count].astype(
            jnp.float32
        )
    return summed


def back_taps(ahead, weight, count):
    final_tap = weight.shape[0] - 1
    summed = jnp.zeros((count, ahead.shape[1]), jnp.float32)
    for offset in range(weight.shape[0]):
        summed = (
            summed
            + weight[offset][None, :] * ahead[final_tap - offset : final_tap - offset + count]
        )
    return summed


def weight_taps(grad_pre, padded, count, tap_count):
    return jnp.stack(
        [
            jnp.sum(grad_pre * padded[offset : offset + count].astype(jnp.float32), axis=0)
            for offset in range(tap_count)
        ]
    )


def decay_table(cum_blocks):
    size_rows = cum_blocks.shape[1]
    row_ids = lax.broadcasted_iota(jnp.int32, (size_rows, size_rows), 0)
    col_ids = lax.broadcasted_iota(jnp.int32, (size_rows, size_rows), 1)
    allowed = (col_ids <= row_ids)[None, :, :, None]
    spread = cum_blocks[:, :, None, :] - cum_blocks[:, None, :, :]
    return jnp.where(allowed, jnp.exp(jnp.where(allowed, spread, 0.0)), 0.0)


def local(
    x_proj, z_proj, b_proj, c_proj, dt_raw, a_log, d_skip, conv_x, conv_bc, norm_gain, grad_out
):
    length = x_proj.shape[0]
    head_count = dt_raw.shape[0]
    row_width = x_proj.shape[1]
    head_dim = row_width // head_count
    state_dim = b_proj.shape[1]
    tap_count = conv_x.shape[0]
    blocks = length // GROUP
    channels = HEADS * HEAD_DIM
    bc_proj = jnp.concatenate([b_proj, c_proj], axis=1)
    edges = passed_along(
        (x_proj[length - tap_count + 1 :], bc_proj[length - tap_count + 1 :]), "ctx", 1
    )
    x_padded = jnp.concatenate([edges[0], x_proj], axis=0)
    bc_padded = jnp.concatenate([edges[1], bc_proj], axis=0)
    x_pre = tap_sum(x_padded, conv_x, length)
    bc_pre = tap_sum(bc_padded, conv_bc, length)
    x_act = jax.nn.silu(x_pre)
    bc_act = jax.nn.silu(bc_pre)
    decay_rate = jnp.exp(a_log)
    step_size = jax.nn.softplus(dt_raw).T
    x_blocks = x_act.reshape(blocks, GROUP, head_count, head_dim)
    b_blocks = bc_act[:, :state_dim].reshape(blocks, GROUP, state_dim)
    c_blocks = bc_act[:, state_dim:].reshape(blocks, GROUP, state_dim)
    d_blocks = step_size.reshape(blocks, GROUP, head_count)
    cum_blocks = jnp.cumsum(
        (-step_size * decay_rate[None, :]).reshape(blocks, GROUP, head_count), axis=1
    )
    block_ends = cum_blocks[:, -1, :]
    block_decay = jnp.exp(block_ends)
    tail_decay = jnp.exp(cum_blocks[:, -1:, :] - cum_blocks)
    tail_weight = tail_decay * d_blocks
    block_states = jnp.einsum(
        "cshp,csn->chpn", tail_weight[..., None] * x_blocks, b_blocks, precision=HIGH
    )

    running = jnp.zeros((head_count, head_dim, state_dim), jnp.float32)
    local_entering = []
    for index in range(blocks):
        local_entering.append(running)
        running = block_decay[index][:, None, None] * running + block_states[index]
    shard_state = running
    local_entering = jnp.stack(local_entering)
    prefix_log = jnp.cumsum(block_ends, axis=0) - block_ends
    shard_decay = jnp.exp(jnp.sum(block_ends, axis=0))

    entering = exclusive_scan(shard_decay, shard_state, "ctx", 1)
    block_entry = jnp.exp(prefix_log)[:, :, None, None] * entering[None] + local_entering

    decay_map = decay_table(cum_blocks)
    scores = jnp.einsum("ctn,csn->cts", c_blocks, b_blocks, precision=HIGH)
    weighted = scores[..., None] * decay_map
    mixing = weighted * d_blocks[:, None, :, :]
    inside = jnp.einsum("ctsh,cshp->cthp", mixing, x_blocks, precision=HIGH)
    carried_raw = jnp.einsum("ctn,chpn->cthp", c_blocks, block_entry, precision=HIGH)
    start_decay = jnp.exp(cum_blocks)
    ssm_blocks = inside + start_decay[..., None] * carried_raw
    skip_rep = jnp.repeat(d_skip, head_dim)
    ssm_out = ssm_blocks.reshape(length, row_width) + skip_rep[None, :] * x_act
    z_float = z_proj.astype(jnp.float32)
    gate_act = jax.nn.silu(z_float)
    gated_out = ssm_out * gate_act
    grad_float = grad_out.astype(jnp.float32)
    scaled_grad = norm_gain[None, :] * grad_float
    norm_sums = lax.psum(
        jnp.stack(
            [jnp.sum(gated_out * gated_out, axis=1), jnp.sum(scaled_grad * gated_out, axis=1)]
        ),
        "head",
    )
    square_sum, cross_sum = norm_sums[0], norm_sums[1]
    inv_rms = lax.rsqrt(square_sum / channels + EPS)[:, None]
    y_out = (gated_out * inv_rms * norm_gain[None, :]).astype(jnp.bfloat16)
    grad_gain_part = jnp.sum(grad_float * gated_out * inv_rms, axis=0)
    grad_gated = inv_rms * scaled_grad - gated_out * (inv_rms * inv_rms * inv_rms) * (
        cross_sum[:, None] / channels
    )
    grad_ssm = grad_gated * gate_act
    grad_z = (grad_gated * ssm_out * silu_grad(z_float)).astype(jnp.bfloat16)
    grad_skip_part = jnp.sum((grad_ssm * x_act).reshape(length, head_count, head_dim), axis=(0, 2))
    grad_blocks = grad_ssm.reshape(blocks, GROUP, head_count, head_dim)
    start_map = start_decay[..., None] * grad_blocks
    local_pull = jnp.einsum("cthp,ctn->chpn", start_map, c_blocks, precision=HIGH)
    shard_pull = jnp.sum(jnp.exp(prefix_log)[:, :, None, None] * local_pull, axis=0)

    leaving = exclusive_scan(shard_decay, shard_pull, "ctx", -1)
    running = leaving
    block_exit = [None] * blocks
    for index in reversed(range(blocks)):
        block_exit[index] = running
        running = block_decay[index][:, None, None] * running + local_pull[index]
    block_exit = jnp.stack(block_exit)

    b_exit = jnp.einsum("csn,chpn->cshp", b_blocks, block_exit, precision=HIGH)
    pulled = (
        jnp.einsum("ctsh,cthp->cshp", weighted, grad_blocks, precision=HIGH)
        + tail_decay[..., None] * b_exit
    )
    grad_x_blocks = d_blocks[..., None] * pulled
    grad_step_blocks = jnp.sum(x_blocks * pulled, axis=3)
    pair_grad = jnp.einsum("cthp,cshp->ctsh", grad_blocks, x_blocks, precision=HIGH)
    masked = pair_grad * decay_map * d_blocks[:, None, :, :]
    grad_scores = jnp.sum(masked, axis=3)
    grad_c_blocks = jnp.einsum("cts,csn->ctn", grad_scores, b_blocks, precision=HIGH)
    grad_b_blocks = jnp.einsum("cts,ctn->csn", grad_scores, c_blocks, precision=HIGH)
    through = masked * scores[..., None]
    grad_cum = jnp.sum(through, axis=2) - jnp.sum(through, axis=1)
    grad_cum = grad_cum + jnp.sum(start_map * carried_raw, axis=3)
    grad_c_blocks = grad_c_blocks + jnp.einsum(
        "cthp,chpn->ctn", start_map, block_entry, precision=HIGH
    )
    release = tail_weight * jnp.sum(x_blocks * b_exit, axis=3)
    grad_cum = grad_cum - release
    end_total = jnp.sum(release, axis=1) + jnp.exp(block_ends) * jnp.sum(
        block_entry * block_exit, axis=(2, 3)
    )
    grad_cum = jnp.concatenate(
        [grad_cum[:, :-1], grad_cum[:, -1:] + end_total[:, None, :]], axis=1
    )
    grad_log_blocks = jnp.flip(jnp.cumsum(jnp.flip(grad_cum, 1), axis=1), 1)
    grad_b_blocks = grad_b_blocks + jnp.einsum(
        "cshp,chpn->csn", tail_weight[..., None] * x_blocks, block_exit, precision=HIGH
    )

    grad_log_rows = grad_log_blocks.reshape(length, head_count)
    grad_step_rows = (
        grad_step_blocks.reshape(length, head_count) - decay_rate[None, :] * grad_log_rows
    )
    grad_alog_part = decay_rate * -jnp.sum(step_size * grad_log_rows, axis=0)
    grad_dt = (grad_step_rows * jax.nn.sigmoid(dt_raw).T).T
    grad_x_act = grad_x_blocks.reshape(length, row_width) + skip_rep[None, :] * grad_ssm
    grad_bc_act = jnp.concatenate(
        [grad_b_blocks.reshape(length, state_dim), grad_c_blocks.reshape(length, state_dim)], axis=1
    )
    grad_x_pre = grad_x_act * silu_grad(x_pre)
    grad_bc_pre = grad_bc_act * silu_grad(bc_pre)
    ahead = passed_along((grad_x_pre[: tap_count - 1], grad_bc_pre[: tap_count - 1]), "ctx", -1)
    x_ahead = jnp.concatenate([grad_x_pre, ahead[0]], axis=0)
    bc_ahead = jnp.concatenate([grad_bc_pre, ahead[1]], axis=0)
    grad_x = back_taps(x_ahead, conv_x, length).astype(jnp.bfloat16)
    bc_back = back_taps(bc_ahead, conv_bc, length)
    shares = lax.psum_scatter(bc_back, "head", scatter_dimension=0, tiled=True)
    grad_b = shares[:, :state_dim].astype(jnp.bfloat16)
    grad_c = shares[:, state_dim:].astype(jnp.bfloat16)
    grad_convx_part = weight_taps(grad_x_pre, x_padded, length, tap_count)
    grad_convbc_part = weight_taps(grad_bc_pre, bc_padded, length, tap_count)

    head_slots = lax.axis_size("head")
    own_slot = lax.axis_index("head")
    per_head = jnp.concatenate(
        [grad_alog_part, grad_skip_part, grad_convx_part.reshape(-1), grad_gain_part]
    )
    slot_mask = (jnp.arange(head_slots) == own_slot).astype(jnp.float32)[:, None]
    slots = (slot_mask * per_head[None, :]).reshape(-1)
    totals = lax.psum(jnp.concatenate([slots, grad_convbc_part.reshape(-1)]), ("ctx", "head"))
    per_size = per_head.shape[0]
    own_total = lax.dynamic_slice_in_dim(totals, own_slot * per_size, per_size)
    grad_alog = own_total[:head_count]
    grad_dskip = own_total[head_count : 2 * head_count]
    convx_size = grad_convx_part.size
    grad_convx = own_total[2 * head_count : 2 * head_count + convx_size].reshape(
        grad_convx_part.shape
    )
    grad_gain = own_total[2 * head_count + convx_size :]
    grad_convbc = totals[head_slots * per_size :].reshape(grad_convbc_part.shape)
    return (
        y_out,
        grad_x,
        grad_z,
        grad_b,
        grad_c,
        grad_dt,
        grad_alog,
        grad_dskip,
        grad_convx,
        grad_convbc,
        grad_gain,
    )


def solution(mesh):
    return jax.shard_map(
        local,
        mesh=mesh,
        in_specs=(
            P("ctx", "head"),
            P("ctx", "head"),
            P("ctx", None),
            P("ctx", None),
            P("head", "ctx"),
            P("head"),
            P("head"),
            P(None, "head"),
            P(),
            P("head"),
            P("ctx", "head"),
        ),
        out_specs=(
            P("ctx", "head"),
            P("ctx", "head"),
            P("ctx", "head"),
            P(("ctx", "head"), None),
            P(("ctx", "head"), None),
            P("head", "ctx"),
            P("head"),
            P("head"),
            P(None, "head"),
            P(),
            P("head"),
        ),
        check_vma=False,
    )
```

time: 679 us -> 513 us (0.76)
  blocking collectives: 206 us -> 34.1 us
  waiting for transfers between devices: 159 us -> 270 us
  local copies, waits for them, and re-layouts: 93.2 us -> 42.6 us
  starting transfers between devices: 115 us -> 68.1 us
  matrix products: 41.9 us -> 32.2 us
    psum x0 -> x1, waiting for transfers between devices: none -> 234 us  [local(): lax.psum(jnp.concatenate([slots, grad_convbc_part.reshape(-1)]), ('ctx',...]
    psum x4 -> x1, blocking collectives: 206 us -> 34.1 us  [local(): lax.psum(jnp.stack([jnp.sum(gated_out * gated_out, axis=1), jnp.sum(scale...]
    ppermute x34 -> x18, waiting for transfers between devices: 159 us -> 36.1 us  [passed_along(): return lax.ppermute(block, axis, route)]
    dynamic_update_slice x12 -> x0, local copies, waits for them, and re-layouts: 50.9 us -> none  [the longest x8 48.2 us: local(): lax.map(forward_block, (x_blocks, b_blocks, c_blocks, d_blocks, cum_block...]
    ppermute x34 -> x18, starting transfers between devices: 115 us -> 68 us  [passed_along(): return lax.ppermute(block, axis, route)]
    dot_general x25 -> x11, matrix products: 40.9 us -> 31.2 us  [the longest x1 8.44 us: local(): jnp.einsum('cthp,cshp->ctsh', grad_blocks, x_blocks, precision=HIGH)]
    unnamed x99 -> x210, local copies, waits for them, and re-layouts: 10.4 us -> 14 us
  transfers between devices with their start and end apart: 35 -> 20, of which waited for: 31 -> 11; matrix products, arithmetic and copies ran while one was open for 4% -> 14% of each run, Pallas kernels for 0% -> 0%
where the time goes in v1:
time: 513 us; the launch traced here: 506 us
  waiting for transfers between devices  270 us (53%)
  starting transfers between devices  68.1 us (13%)
  local copies, waits for them, and re-layouts  42.6 us (8%)
  other arithmetic  42.1 us (8%)
  blocking collectives  34.1 us (7%)
  matrix products  32.2 us (6%)
  between operations  17.4 us (3%)
    psum x1, waiting for transfers between devices, local(): lax.psum(jnp.concatenate([slots, grad_convbc_part.reshape(-1)]), ('ctx',...  234 us
    ppermute x18, starting transfers between devices, passed_along(): return lax.ppermute(block, axis, route)  68 us
    ppermute x18, waiting for transfers between devices, passed_along(): return lax.ppermute(block, axis, route)  36.1 us
    psum x1, blocking collectives, local(): lax.psum(jnp.stack([jnp.sum(gated_out * gated_out, axis=1), jnp.sum(scale...  34.1 us
    unnamed x210, local copies, waits for them, and re-layouts  14 us
  transfers between devices with their start and end apart: 20, of which 11 were waited for; matrix products, arithmetic and copies ran while one was open for 14% of the time, Pallas kernels for 0%

profile of v1, /device:TPU:1, one launch (start us, length us, event | category | flops | bytes accessed | tf_op | source)
XLA Modules:
  0.0 506.2 jit_solution(17537154656387254641)
XLA Ops:
  8.9 4.9 collective-permute-start
  28.5 2.9 reshape.185
  34.2 3.9 collective-permute-start.5
  38.1 3.3 collective-permute-done.5
  42.2 3.6 collective-permute-start.6
  45.8 3.1 collective-permute-start.9
  48.9 3.4 collective-permute-start.2
  54.4 7.1 %collective-permute-start.7 = (f32[8,64,128]{2,1,0:T(8,128)}, f32[8,64,128]{2,1,0:T(8,128)}, u32[]{:S(2)}, u32[]{:S(2)}) collective-permute-start(f32[8,64,128]{2,1,0:T(8,128)} %multiply_add_fusion.5), channel_id=1, source_target_pairs={{0,64},{16,80},{32,96},{48,112},{64,128},{80,144},{96,160},{112,17... | collective-permute-start | bytes 786440 | tf_op jit(solution)/shard_map/ppermute | solution.py:18
  72.1 4.0 collective-permute-start.4
  78.1 6.8 %collective-permute-start.8 = (f32[8,64,128]{2,1,0:T(8,128)S(1)}, f32[8,64,128]{2,1,0:T(8,128)S(1)}, u32[]{:S(2)}, u32[]{:S(2)}) collective-permute-start(f32[8,64,128]{2,1,0:T(8,128)S(1)} %multiply_add_fusion.4), channel_id=1, source_target_pairs={{0,128},{16,144},{32,160},{48,176},{64,192},{80,208},{96,224},{112... | collective-permute-start | bytes 786440 | tf_op jit(solution)/shard_map/ppermute | solution.py:18
  90.9 3.9 fusion.24
  99.1 34.1 %psum.14 = f32[2,512]{1,0:T(2,128)} all-reduce(f32[2,512]{1,0:T(2,128)} %pad_maximum_fusion.9), channel_id=1, replica_groups=mesh['ctx'=16,'head'=16] {'head'}, use_global_device_ids=true, to_apply=%region_6.7 | all-reduce | flops 1024 | bytes 8192 | tf_op jit(solution)/shard_map/psum | solution.py:147
  134.0 4.7 multiply_reduce_fusion.2
  140.6 3.5 multiply_reduce_fusion.8
  144.1 14.1 %collective-permute-start.12 = (f32[8,64,128]{2,1,0:T(8,128)}, f32[8,64,128]{2,1,0:T(8,128)}, u32[]{:S(2)}, u32[]{:S(2)}) collective-permute-start(f32[8,64,128]{2,1,0:T(8,128)} %get-tuple-element.140), channel_id=1, source_target_pairs={{16,0},{32,16},{48,32},{64,48},{80,64},{96,80},{112,96},{128,112},... | collective-permute-start | bytes 786440 | tf_op jit(solution)/shard_map/ppermute | solution.py:18
  158.2 4.7 collective-permute-done.12
  169.4 5.2 %collective-permute-done.10 = f32[8]{0:T(128)S(1)} collective-permute-done((f32[8]{0:T(128)}, f32[8]{0:T(128)S(1)}, u32[]{:S(2)}, u32[]{:S(2)}) %collective-permute-start.10) | collective-permute-done | bytes 64 | tf_op jit(solution)/shard_map/ppermute | solution.py:18
  176.6 5.0 collective-permute-done.11
  185.6 8.4 %multiply_reduce_fusion = (f32[2,256,8]{1,2,0:T(8,128)}, f32[2,256,8]{1,2,0:T(8,128)}, f32[2,256,256]{1,2,0:T(8,128)}) fusion(f32[2,256,256]{1,2,0:T(8,128)} %copy-done.35, f32[2,256,8]{1,2,0:T(8,128)} %bitcast.181, f32[2,256,8]{1,2,0:T(8,128)} %copy.174, pred[256,256]{0,1:T(8,128)(4,1)} %iota_compare_fusion, f32[2,256,8,64]{1,0,3,2:T(2,128)S(1)} %reshape.192, ...), kind=kOutput, calls=%fused_computation.7 | convolution fusion | flops 814604288 | bytes 3276800 | tf_op jit(solution)/shard_map/cthp,cshp->ctsh/dot_general | solution.py:183
  194.8 7.3 %collective-permute-done.14 = f32[8,64,128]{2,1,0:T(8,128)S(1)} collective-permute-done((f32[8,64,128]{2,1,0:T(8,128)S(1)}, f32[8,64,128]{2,1,0:T(8,128)S(1)}, u32[]{:S(2)}, u32[]{:S(2)}) %collective-permute-start.14) | collective-permute-done | bytes 262176 | tf_op jit(solution)/shard_map/ppermute | solution.py:18
  224.7 3.6 collective-permute-start.17
  228.4 5.4 %multiply_reduce_fusion.3 = (f32[2,256,8]{1,2,0:T(8,128)}, f32[2,256,8]{1,2,0:T(8,128)}, f32[2,256,8,64]{1,3,2,0:T(8,128)S(1)}) fusion(f32[2,256,8,64]{1,3,2,0:T(8,128)S(1)} %fusion.91, f32[2,256,8,64]{1,0,3,2:T(2,128)S(1)} %copy-done.11, f32[2,256,8]{1,2,0:T(8,128)S(1)} %bitcast.183, f32[2,256,8]{1,2,0:T(8,128)S(1)} %copy-done.60, ...), kind=kOutput, calls=%fused_computation.76 | convolution fusion | flops 811327488 | bytes 4866048 | tf_op jit(solution)/shard_map/ctsh,cthp->cshp/dot_general | solution.py:178
  249.6 6.0 %collective-permute-done.16 = f32[3,512]{0,1:T(8,128)S(1)} collective-permute-done((f32[3,512]{0,1:T(8,128)S(1)}, f32[3,512]{0,1:T(8,128)S(1)}, u32[]{:S(2)}, u32[]{:S(2)}) %collective-permute-start.16) | collective-permute-done | bytes 6176 | tf_op jit(solution)/shard_map/ppermute | solution.py:18
  258.1 233.6 %all-reduce.3.cloned.1.call-done = f32[42240]{0:T(1024)} async-done(((f32[42240]{0:T(1024)}), f32[42240]{0:T(1024)}) %all-reduce.3.cloned.1.call-update) | async-done | bytes 168976 | tf_op jit(solution)/shard_map/psum | solution.py:237
  (344 shorter events, 106.2 us)
Async XLA Ops:
  8.0 483.6 %all-reduce.3.cloned.1.call-start = ((), (), s32[]{:S(2)}) async-start(), calls=%async_computation.2 | async-start | bytes 344064 | tf_op jit(solution)/shard_map/psum | solution.py:237
  8.9 17.5 %collective-permute-start = (bf16[3,512]{0,1:T(8,128)(2,1)S(1)}, bf16[3,512]{0,1:T(8,128)(2,1)S(1)}, u32[]{:S(2)}, u32[]{:S(2)}) collective-permute-start(bf16[3,512]{0,1:T(8,128)(2,1)S(1)} %copy.169), channel_id=1, source_target_pairs={{0,16},{16,32},{32,48},{48,64},{64,80},{80,96},{96,112},{112,128},... | collective-permute-start | bytes 9224 | tf_op jit(solution)/shard_map/ppermute | solution.py:18
  15.8 9.9 %collective-permute-start.1 = (bf16[3,256]{1,0:T(4,128)(2,1)S(1)}, bf16[3,256]{1,0:T(4,128)(2,1)S(1)}, u32[]{:S(2)}, u32[]{:S(2)}) collective-permute-start(bf16[3,256]{1,0:T(4,128)(2,1)S(1)} %slice.221), channel_id=1, source_target_pairs={{0,16},{16,32},{32,48},{48,64},{64,80},{80,96},{96,112},{112,128},... | collective-permute-start | bytes 4616 | tf_op jit(solution)/shard_map/ppermute | solution.py:18
  23.4 38.8 %copy-start.17 = (f32[2,8,256]{1,0,2:T(2,128)}, f32[2,8,256]{1,0,2:T(2,128)S(1)}, u32[]{:S(2)}) copy-start(f32[2,8,256]{1,0,2:T(2,128)S(1)} %copy.173) | copy-start | bytes 49156
  26.4 62.7 %copy-start.1 = (f32[512,128]{1,0:T(8,128)}, f32[512,128]{1,0:T(8,128)S(1)}, u32[]{:S(2)}) copy-start(f32[512,128]{1,0:T(8,128)S(1)} %get-tuple-element.114) | copy-start | bytes 786436
  34.2 7.2 %collective-permute-start.5 = (f32[8,64,128]{2,1,0:T(8,128)S(1)}, f32[8,64,128]{2,1,0:T(8,128)S(1)}, u32[]{:S(2)}, u32[]{:S(2)}) collective-permute-start(f32[8,64,128]{2,1,0:T(8,128)S(1)} %fusion.96), channel_id=1, source_target_pairs={{0,16},{16,32},{32,48},{48,64},{64,80},{80,96},{96,112},{112,128},... | collective-permute-start | bytes 786440 | tf_op jit(solution)/shard_map/ppermute | solution.py:18
  38.1 23.5 %copy-start.93 = (f32[8]{0:T(128)}, f32[8]{0:T(128)S(1)}, u32[]{:S(2)}) copy-start(f32[8]{0:T(128)S(1)} %exp.62) | copy-start | bytes 100
  38.1 24.8 %copy-start.97 = (f32[8]{0:T(128)S(1)}, f32[8]{0:T(128)}, u32[]{:S(2)}) copy-start(f32[8]{0:T(128)} %param.17) | copy-start | bytes 100
  42.2 11.4 %collective-permute-start.6 = (f32[8,64,128]{2,1,0:T(8,128)S(1)}, f32[8,64,128]{2,1,0:T(8,128)S(1)}, u32[]{:S(2)}, u32[]{:S(2)}) collective-permute-start(f32[8,64,128]{2,1,0:T(8,128)S(1)} %multiply_add_fusion.6), channel_id=1, source_target_pairs={{0,32},{16,48},{32,64},{48,80},{64,96},{80,112},{96,128},{112,144}... | collective-permute-start | bytes 786440 | tf_op jit(solution)/shard_map/ppermute | solution.py:18
  45.8 6.6 %collective-permute-start.9 = (f32[8]{0:T(128)S(1)}, f32[8]{0:T(128)S(1)}, u32[]{:S(2)}, u32[]{:S(2)}) collective-permute-start(f32[8]{0:T(128)S(1)} %exp.62), channel_id=1, source_target_pairs={{16,0},{32,16},{48,32},{64,48},{80,64},{96,80},{112,96},{128,112},... | collective-permute-start | bytes 104 | tf_op jit(solution)/shard_map/ppermute | solution.py:18
  48.9 4.1 collective-permute-start.2
  54.4 22.4 %collective-permute-start.7 = (f32[8,64,128]{2,1,0:T(8,128)}, f32[8,64,128]{2,1,0:T(8,128)}, u32[]{:S(2)}, u32[]{:S(2)}) collective-permute-start(f32[8,64,128]{2,1,0:T(8,128)} %multiply_add_fusion.5), channel_id=1, source_target_pairs={{0,64},{16,80},{32,96},{48,112},{64,128},{80,144},{96,160},{112,17... | collective-permute-start | bytes 786440 | tf_op jit(solution)/shard_map/ppermute | solution.py:18
  68.9 3.3 collective-permute-start.3
  72.1 4.7 collective-permute-start.4
  78.1 9.9 %collective-permute-start.8 = (f32[8,64,128]{2,1,0:T(8,128)S(1)}, f32[8,64,128]{2,1,0:T(8,128)S(1)}, u32[]{:S(2)}, u32[]{:S(2)}) collective-permute-start(f32[8,64,128]{2,1,0:T(8,128)S(1)} %multiply_add_fusion.4), channel_id=1, source_target_pairs={{0,128},{16,144},{32,160},{48,176},{64,192},{80,208},{96,224},{112... | collective-permute-start | bytes 786440 | tf_op jit(solution)/shard_map/ppermute | solution.py:18
  144.1 18.8 %collective-permute-start.12 = (f32[8,64,128]{2,1,0:T(8,128)}, f32[8,64,128]{2,1,0:T(8,128)}, u32[]{:S(2)}, u32[]{:S(2)}) collective-permute-start(f32[8,64,128]{2,1,0:T(8,128)} %get-tuple-element.140), channel_id=1, source_target_pairs={{16,0},{32,16},{48,32},{64,48},{80,64},{96,80},{112,96},{128,112},... | collective-permute-start | bytes 786440 | tf_op jit(solution)/shard_map/ppermute | solution.py:18
  164.7 18.1 %collective-permute-start.13 = (f32[8,64,128]{2,1,0:T(8,128)}, f32[8,64,128]{2,1,0:T(8,128)}, u32[]{:S(2)}, u32[]{:S(2)}) collective-permute-start(f32[8,64,128]{2,1,0:T(8,128)} %multiply_add_fusion.3), channel_id=1, source_target_pairs={{32,0},{48,16},{64,32},{80,48},{96,64},{112,80},{128,96},{144,112}... | collective-permute-start | bytes 786440 | tf_op jit(solution)/shard_map/ppermute | solution.py:18
  168.2 6.5 %collective-permute-start.10 = (f32[8]{0:T(128)}, f32[8]{0:T(128)S(1)}, u32[]{:S(2)}, u32[]{:S(2)}) collective-permute-start(f32[8]{0:T(128)} %get-tuple-element.138), channel_id=1, source_target_pairs={{32,0},{48,16},{64,32},{80,48},{96,64},{112,80},{128,96},{144,112}... | collective-permute-start | bytes 104 | tf_op jit(solution)/shard_map/ppermute | solution.py:18
  175.4 6.3 %collective-permute-start.11 = (f32[8]{0:T(128)S(1)}, f32[8]{0:T(128)S(1)}, u32[]{:S(2)}, u32[]{:S(2)}) collective-permute-start(f32[8]{0:T(128)S(1)} %mul.688), channel_id=1, source_target_pairs={{64,0},{80,16},{96,32},{112,48},{128,64},{144,80},{160,96},{176,11... | collective-permute-start | bytes 104 | tf_op jit(solution)/shard_map/ppermute | solution.py:18
  183.9 18.2 %collective-permute-start.14 = (f32[8,64,128]{2,1,0:T(8,128)S(1)}, f32[8,64,128]{2,1,0:T(8,128)S(1)}, u32[]{:S(2)}, u32[]{:S(2)}) collective-permute-start(f32[8,64,128]{2,1,0:T(8,128)S(1)} %multiply_add_fusion.2), channel_id=1, source_target_pairs={{64,0},{80,16},{96,32},{112,48},{128,64},{144,80},{160,96},{176,11... | collective-permute-start | bytes 786440 | tf_op jit(solution)/shard_map/ppermute | solution.py:18
  203.0 13.6 %collective-permute-start.15 = (f32[8,64,128]{2,1,0:T(8,128)}, f32[8,64,128]{2,1,0:T(8,128)}, u32[]{:S(2)}, u32[]{:S(2)}) collective-permute-start(f32[8,64,128]{2,1,0:T(8,128)} %multiply_add_fusion.1), channel_id=1, source_target_pairs={{128,0},{144,16},{160,32},{176,48},{192,64},{208,80},{224,96},{240... | collective-permute-start | bytes 786440 | tf_op jit(solution)/shard_map/ppermute | solution.py:18
  224.7 18.8 %collective-permute-start.17 = (f32[3,256]{1,0:T(4,128)}, f32[3,256]{1,0:T(4,128)}, u32[]{:S(2)}, u32[]{:S(2)}) collective-permute-start(f32[3,256]{1,0:T(4,128)} %slice.241), channel_id=1, source_target_pairs={{16,0},{32,16},{48,32},{64,48},{80,64},{96,80},{112,96},{128,112},... | collective-permute-start | bytes 9224 | tf_op jit(solution)/shard_map/ppermute | solution.py:18
  243.5 253.5 %reduce-scatter.2.cloned.1.call-start = ((), (), s32[]{:S(2)}) async-start(), calls=%async_computation.1 | async-start | bytes 557056 | tf_op jit(solution)/shard_map/reduce_scatter | solution.py:224
  245.5 10.1 %collective-permute-start.16 = (f32[3,512]{0,1:T(8,128)S(1)}, f32[3,512]{0,1:T(8,128)S(1)}, u32[]{:S(2)}, u32[]{:S(2)}) collective-permute-start(f32[3,512]{0,1:T(8,128)S(1)} %slice.236), channel_id=1, source_target_pairs={{16,0},{32,16},{48,32},{64,48},{80,64},{96,80},{112,96},{128,112},... | collective-permute-start | bytes 18440 | tf_op jit(solution)/shard_map/ppermute | solution.py:18
  (95 other events, 427.6 us)
Sparse Core Ops, SparseCore 0:
  243.6 247.9 all-reduce.2
Sparse Core Ops, SparseCore 1:
  247.4 75.8 reduce-scatter.1
